TPU v7x, 32 devices: a whole 2x2x4 slice. The times are simulated.
32 devices in a mesh: gx: 2 (over core), gy: 2 (over x), gz: 8 (over z, y).
Axes of the slice: x: 2, y: 2, z: 4, core: 2. Of those that a mesh axis runs over, the one named last changes fastest.
Arguments:
- charges: bfloat16 [32, 48, 2048], P('gx', 'gy', 'gz'), may hold values from -6 to 6
- kernel_fine: bfloat16 [9, 9, 9], replicated, may hold values from -0.21875 to 0.21875
- kernel_mid: bfloat16 [9, 9, 9], replicated, may hold values from -0.21875 to 0.21875
- gauss_width: float32 [8], replicated, may hold values from 1 to 64
- gauss_weight: float32 [8], replicated, may hold values from 0.25 to 2
Outputs:
- potential: float32 [32, 48, 2048], P('gx', 'gy', 'gz')
All inputs are finite; a program needn't handle non-finite values.
Results may differ from a plain program's by a relative error of at most 0.002.
Values may be sent and summed in bfloat16 or wider, within the bound.
No kernel may reach another device: no remote copies, remote signals or barrier semaphores. Data moves between devices by JAX's collectives and lax.ppermute only.
A program may use at most 384 MiB of HBM per device.

v0:
```python
import jax
import jax.numpy as jnp
from jax import lax
from jax.sharding import PartitionSpec as P

M = 16


def padded_2(cells, sides, width):
    for axis, dim in sides:
        count = lax.axis_size(axis)
        ends = count - 1
        head = lax.slice_in_dim(cells, 0, width, axis=dim)
        tail = lax.slice_in_dim(cells, cells.shape[dim] - width, cells.shape[dim], axis=dim)
        cells = jnp.concatenate(
            [
                lax.ppermute(tail, axis, [(i, (i + 1) % count) for i in range(ends)]),
                cells,
                lax.ppermute(head, axis, [((i + 1) % count, i) for i in range(ends)]),
            ],
            axis=dim,
        )
    return cells


def stencil(offset):
    value = jnp.zeros(offset.shape, jnp.float32)
    value = jnp.where(jnp.abs(offset) == 1, 9.0 / 16.0, value)
    value = jnp.where(offset == 0, 1.0, value)
    value = jnp.where(jnp.abs(offset) == 3, -1.0 / 16.0, value)
    return value


def restrict_band(rows, cols, margin):
    row_ids = jnp.arange(rows, dtype=jnp.int32)[:, None]
    col_ids = jnp.arange(cols, dtype=jnp.int32)[None, :]
    return stencil(col_ids - margin - 2 * row_ids)


def prolong_band(rows, cols):
    row_ids = jnp.arange(rows, dtype=jnp.int32)[:, None]
    col_ids = jnp.arange(cols, dtype=jnp.int32)[None, :]
    return stencil(row_ids - 2 * col_ids + 4)


def restrict_padded(padded, sizes, margin):
    highest = lax.Precision.HIGHEST
    band_x = restrict_band(sizes[0], padded.shape[0], margin).astype(jnp.bfloat16)
    band_y = restrict_band(sizes[1], padded.shape[1], margin)
    band_z = restrict_band(sizes[2], padded.shape[2], margin)
    field = jnp.einsum("ia,abcm->ibcm", band_x, padded, preferred_element_type=jnp.float32)
    field = jnp.einsum("jb,ibcm->ijcm", band_y, field, precision=highest)
    field = jnp.einsum("kc,ijcm->ijkm", band_z, field, precision=highest)
    return field


def prolong_ext(field, sizes):
    highest = lax.Precision.HIGHEST
    field = jnp.einsum(
        "ia,abcm->ibcm", prolong_band(sizes[0], field.shape[0]), field, precision=highest
    )
    field = jnp.einsum(
        "jb,ibcm->ijcm", prolong_band(sizes[1], field.shape[1]), field, precision=highest
    )
    field = jnp.einsum(
        "kc,ijcm->ijkm", prolong_band(sizes[2], field.shape[2]), field, precision=highest
    )
    return field


def correlate(padded, kernel, out_sizes):
    reach = jnp.arange(9, dtype=jnp.int32)[:, None, None]
    lag_y = (
        jnp.arange(padded.shape[1], dtype=jnp.int32)[:, None]
        - jnp.arange(out_sizes[1], dtype=jnp.int32)[None, :]
    )
    lag_z = (
        jnp.arange(padded.shape[2], dtype=jnp.int32)[:, None]
        - jnp.arange(out_sizes[2], dtype=jnp.int32)[None, :]
    )
    pick_y = (lag_y[None] == reach).astype(jnp.bfloat16)
    pick_z = (lag_z[None] == reach).astype(jnp.bfloat16)
    total = jnp.zeros((out_sizes[0], out_sizes[1], out_sizes[2], padded.shape[3]), jnp.float32)
    for offset in range(9):
        table = jnp.einsum(
            "bc,bpy,cqz->pqyz", kernel[offset], pick_y, pick_z, preferred_element_type=jnp.float32
        ).astype(jnp.bfloat16)
        total = total + jnp.einsum(
            "xpqm,pqyz->xyzm",
            padded[offset : offset + out_sizes[0]],
            table,
            preferred_element_type=jnp.float32,
        )
    return total


def gaussian_table(first_row, rows, cols, whole, gauss_width):
    row_pos = first_row + jnp.arange(rows, dtype=jnp.int32)
    col_pos = jnp.arange(cols, dtype=jnp.int32)
    spread = (row_pos[:, None] - col_pos[None, :]).astype(jnp.float32)
    width = gauss_width[:, None, None]
    table = jnp.exp(-jnp.square(spread[None] / width)) / jnp.sqrt(width)
    inside = (row_pos >= 0) & (row_pos < whole)
    return jnp.where(inside[None, :, None], table, 0.0)


def inside_mask(position, count, local, rim):
    spots = position * local - rim + jnp.arange(local + 2 * rim, dtype=jnp.int32)
    return ((spots >= 0) & (spots < local * count)).astype(jnp.float32)


def per_device(charges, kernel_fine, kernel_mid, gauss_width, gauss_weight):
    highest = lax.Precision.HIGHEST
    size_x, size_y, flat = charges.shape
    members = M
    size_z = flat // members
    field = charges.reshape(size_x, size_y, size_z, members)
    padded = padded_2(field, (("gx", 0), ("gy", 1), ("gz", 2)), 4)
    short_fine = correlate(padded, kernel_fine, (size_x, size_y, size_z))
    mid_sizes = (size_x // 2, size_y // 2, size_z // 2)
    q_mid = restrict_padded(padded, mid_sizes, 4).astype(jnp.bfloat16)
    mid_padded = padded_2(q_mid, (("gx", 0), ("gy", 1), ("gz", 2)), 6)
    short_mid = correlate(
        mid_padded, kernel_mid, (mid_sizes[0] + 4, mid_sizes[1] + 4, mid_sizes[2] + 4)
    )
    top_x, top_y, top_z = (size_x // 4, size_y // 4, size_z // 4)
    q_top = restrict_padded(mid_padded, (top_x, top_y, top_z), 6)
    count_x = lax.axis_size("gx")
    count_y = lax.axis_size("gy")
    count_z = lax.axis_size("gz")
    index_x = lax.axis_index("gx")
    index_y = lax.axis_index("gy")
    index_z = lax.axis_index("gz")
    whole_x = top_x * count_x
    whole_y = top_y * count_y
    whole_z = top_z * count_z
    first_x = index_x * top_x - 3
    first_y = index_y * top_y - 3
    first_z = index_z * top_z - 3
    scaled = gauss_weight[:, None, None]
    piece = lax.all_gather(q_top, "gx", axis=0, tiled=True)
    table = gaussian_table(first_x, top_x + 6, piece.shape[0], whole_x, gauss_width) * scaled
    section = jnp.einsum("gia,abcm->gibcm", table, piece, precision=highest)
    piece = lax.all_gather(section, "gy", axis=2, tiled=True)
    table = gaussian_table(first_y, top_y + 6, piece.shape[2], whole_y, gauss_width)
    section = jnp.einsum("gjb,gibcm->gijcm", table, piece, precision=highest)
    piece = lax.all_gather(section, "gz", axis=3, tiled=True)
    table = gaussian_table(first_z, top_z + 6, piece.shape[3], whole_z, gauss_width)
    section = jnp.einsum("gkc,gijcm->gijkm", table, piece, precision=highest)
    phi_top = jnp.sum(section, axis=0)
    ext_sizes = (mid_sizes[0] + 4, mid_sizes[1] + 4, mid_sizes[2] + 4)
    phi_mid = short_mid + prolong_ext(phi_top, ext_sizes)
    mask_x = inside_mask(index_x, count_x, mid_sizes[0], 2)
    mask_y = inside_mask(index_y, count_y, mid_sizes[1], 2)
    mask_z = inside_mask(index_z, count_z, mid_sizes[2], 2)
    phi_mid = (
        phi_mid
        * mask_x[:, None, None, None]
        * mask_y[None, :, None, None]
        * mask_z[None, None, :, None]
    )
    potential = short_fine + prolong_ext(phi_mid, (size_x, size_y, size_z))
    return potential.reshape(size_x, size_y, size_z * members)


def solution(mesh):
    placed = (P("gx", "gy", "gz"), P(), P(), P(), P())
    return jax.shard_map(
        per_device, mesh=mesh, in_specs=placed, out_specs=P("gx", "gy", "gz"), check_vma=False
    )
```

profile of v0, /device:TPU:0, one launch (start us, length us, event | category | flops | bytes accessed | tf_op | source)
XLA Modules:
  0.0 811.1 jit_solution(4082454548919218295)
XLA Ops:
  51.9 3.7 copy.19
  55.6 4.9 collective-permute-start.2
  60.5 2.9 copy.20
  64.7 3.8 copy.116
  68.5 3.6 copy.120
  72.2 2.6 copy.124
  74.8 3.8 copy.128
  78.6 3.7 copy.132
  85.0 3.7 copy.140
  88.7 3.7 copy.144
  92.4 2.7 copy.112
  95.0 3.9 copy.21
  99.0 4.6 copy.22
  105.5 3.5 collective-permute-start.4
  110.3 16.5 %collective-permute-done.4 = bf16[24,32,4,16]{1,3,2,0:T(8,128)(2,1)S(1)} collective-permute-done((bf16[24,32,4,16]{1,3,2,0:T(8,128)(2,1)S(1)}, bf16[24,32,4,16]{1,3,2,0:T(8,128)(2,1)S(1)}, u32[]{:S(2)}, u32[]{:S(2)}) %collective-permute-start.4) | collective-permute-done | bytes 98336 | tf_op jit(solution)/shard_map/ppermute | solution.py:17
  130.9 7.8 fusion.60
  138.7 7.4 fusion.212
  150.2 6.8 fusion.10
  157.1 4.9 fusion.12
  162.0 4.9 fusion.14
  166.9 4.8 fusion.16
  171.7 4.8 fusion.18
  176.5 5.1 fusion.6
  181.8 4.7 collective-permute-start.8
  187.8 4.8 fusion.8
  192.6 4.5 collective-permute-done.9
  200.6 5.2 collective-permute-start.10
  209.5 6.0 fusion.4
  215.5 10.6 %collective-permute-done.10 = bf16[20,24,6,16]{1,3,2,0:T(8,128)(2,1)} collective-permute-done((bf16[20,24,6,16]{1,3,2,0:T(8,128)(2,1)S(1)}, bf16[20,24,6,16]{1,3,2,0:T(8,128)(2,1)}, u32[]{:S(2)}, u32[]{:S(2)}) %collective-permute-start.10) | collective-permute-done | bytes 92192 | tf_op jit(solution)/shard_map/ppermute | solution.py:17
  231.2 5.7 pad_maximum_fusion
  236.9 6.0 copy.65
  245.0 4.7 convolution_bitcast_fusion.2
  253.4 37.3 %all_gather.10 = f32[8,10,12,4,16]{4,1,3,2,0:T(8,128)S(1)} all-gather(f32[8,10,6,4,16]{4,1,3,2,0:T(8,128)S(1)} %fusion.98), channel_id=1, replica_groups=mesh['gx'=2,'gy'=2,'gz'=8] {'gy'}, dimensions={2}, use_global_device_ids=true | all-gather | bytes 368640 | tf_op jit(solution)/shard_map/all_gather | solution.py:144
  290.8 6.8 fusion.33
  297.6 3.2 fusion.52
  314.3 385.5 %all-gather.2.cloned.1.call-done = f32[8,10,12,32,16]{2,4,3,1,0:T(8,128)} async-done(((f32[8,10,12,4,16]{2,4,3,1,0:T(8,128)}), f32[8,10,12,32,16]{2,4,3,1,0:T(8,128)}) %all-gather.2.cloned.1.call-update) | async-done | bytes 1966096 | tf_op jit(solution)/shard_map/all_gather | solution.py:147
  699.9 26.4 %copy.70 = f32[8,10,12,32,16]{4,3,0,2,1:T(8,128)} copy(f32[8,10,12,32,16]{2,4,3,1,0:T(8,128)} %all-gather.2.cloned.1.call-done) | data formatting | bytes 3932160 | tf_op jit(solution)/shard_map/all_gather | solution.py:147
  726.3 28.3 %convolution_bitcast_fusion = f32[10,12,10,16]{2,3,1,0:T(8,128)} fusion(f32[8,10,12,32,16]{4,3,0,2,1:T(8,128)} %copy.70, f32[8]{0:T(128)S(1)} %sqrt.6, f32[8]{0:T(128)S(1)} %copy-done.26, f32[10,32]{1,0:T(8,128)S(1)} %subtract_convert_fusion, pred[10]{0:T(512)(128)(4,1)S(1)} %compare_and_fusion), kind=kOutput, calls=%fused_computation.105 | convolution fusion | flops 58995200 | bytes 2044234 | tf_op jit(solution)/shard_map/gkc,gijcm->gijkm/dot_general | solution.py:149
  754.6 3.3 copy.71
  760.1 3.0 convolution_bitcast_fusion.1
  763.1 3.6 copy.73
  766.7 3.9 fusion.176
  770.6 3.9 copy.74
  774.5 5.7 fusion.75
  780.2 2.9 fusion.38
  783.1 2.7 copy.76
  789.5 9.7 %bitcast_add_fusion = f32[16,24,16,16]{1,3,0,2:T(8,128)} fusion(f32[24,16,16,16,1]{0,3,4,2,1:T(8,128)} %fusion.4, f32[24,16,16,16,1]{0,3,4,2,1:T(8,128)} %fusion.6, f32[24,16,16,16,1]{0,3,4,2,1:T(8,128)} %fusion.8, f32[24,16,16,16,1]{0,3,4,2,1:T(8,128)S(1)} %copy-done.28, f32[24,16,16,16,1]{0,3,4,2,1:T(8,128)} %fusion.12, ...), kind=kOutput, calls=%fused_computation.33 | convolution fusion | flops 151879680 | bytes 11272192 | tf_op jit(solution)/shard_map/xpqm,pqyz->xyzm/dot_general | solution.py:88
  799.3 2.6 copy.78
  (157 shorter events, 101.4 us)
Async XLA Ops:
  6.5 7.5 copy-start.24
  6.5 693.3 %all-gather.2.cloned.1.call-start = ((), (), s32[]{:S(2)}) async-start(), calls=%async_computation | async-start | bytes 23592960 | tf_op jit(solution)/shard_map/all_gather | solution.py:147
  7.6 42.0 %collective-permute-start = (bf16[4,24,16,16]{1,3,2,0:T(8,128)(2,1)S(1)}, bf16[4,24,16,16]{1,3,2,0:T(8,128)(2,1)S(1)}, u32[]{:S(2)}, u32[]{:S(2)}) collective-permute-start(bf16[4,24,16,16]{1,3,2,0:T(8,128)(2,1)S(1)} %bitcast.636), channel_id=1, source_target_pairs={{0,16},{1,17},{2,18},{3,19},{4,20},{5,21},{6,22},{7,23},{8,24},{9,... | collective-permute-start | bytes 147464 | tf_op jit(solution)/shard_map/ppermute | solution.py:17
  10.2 39.4 %collective-permute-start.1 = (bf16[4,24,16,16]{1,3,2,0:T(8,128)(2,1)S(1)}, bf16[4,24,16,16]{1,3,2,0:T(8,128)(2,1)S(1)}, u32[]{:S(2)}, u32[]{:S(2)}) collective-permute-start(bf16[4,24,16,16]{1,3,2,0:T(8,128)(2,1)S(1)} %bitcast.637), channel_id=1, source_target_pairs={{16,0},{17,1},{18,2},{19,3},{20,4},{21,5},{22,6},{23,7},{24,8},{25... | collective-permute-start | bytes 147464 | tf_op jit(solution)/shard_map/ppermute | solution.py:19
  22.8 5.5 copy-start.25
  44.3 4.7 copy-start.23
  51.9 12.8 %copy-start.26 = (f32[8]{0:T(128)S(1)}, f32[8]{0:T(128)}, u32[]{:S(2)}) copy-start(f32[8]{0:T(128)} %param.8) | copy-start | bytes 100
  55.6 39.5 %collective-permute-start.2 = (bf16[24,4,16,16]{0,3,2,1:T(8,128)(2,1)S(1)}, bf16[24,4,16,16]{0,3,2,1:T(8,128)(2,1)}, u32[]{:S(2)}, u32[]{:S(2)}) collective-permute-start(bf16[24,4,16,16]{0,3,2,1:T(8,128)(2,1)S(1)} %copy.19), channel_id=1, source_target_pairs={{0,8},{1,9},{2,10},{3,11},{4,12},{5,13},{6,14},{7,15},{16,24},{17,... | collective-permute-start | bytes 147464 | tf_op jit(solution)/shard_map/ppermute | solution.py:17
  63.4 35.6 %collective-permute-start.3 = (bf16[24,4,16,16]{0,3,2,1:T(8,128)(2,1)}, bf16[24,4,16,16]{0,3,2,1:T(8,128)(2,1)}, u32[]{:S(2)}, u32[]{:S(2)}) collective-permute-start(bf16[24,4,16,16]{0,3,2,1:T(8,128)(2,1)} %copy.20), channel_id=1, source_target_pairs={{8,0},{9,1},{10,2},{11,3},{12,4},{13,5},{14,6},{15,7},{24,16},{25,... | collective-permute-start | bytes 147464 | tf_op jit(solution)/shard_map/ppermute | solution.py:19
  64.7 7.5 copy-start.6
  74.8 7.5 copy-start.5
  85.0 7.4 copy-start.4
  103.6 23.2 %copy-start = (bf16[24,4,16,16]{1,3,2,0:T(8,128)(2,1)S(1)}, bf16[24,4,16,16]{1,3,2,0:T(8,128)(2,1)}, u32[]{:S(2)}) copy-start(bf16[24,4,16,16]{1,3,2,0:T(8,128)(2,1)} %copy.22) | copy-start | bytes 147460
  105.5 21.2 %collective-permute-start.4 = (bf16[24,32,4,16]{1,3,2,0:T(8,128)(2,1)S(1)}, bf16[24,32,4,16]{1,3,2,0:T(8,128)(2,1)S(1)}, u32[]{:S(2)}, u32[]{:S(2)}) collective-permute-start(bf16[24,32,4,16]{1,3,2,0:T(8,128)(2,1)S(1)} %get-tuple-element.5), channel_id=1, source_target_pairs={{0,1},{1,2},{2,3},{3,4},{4,5},{5,6},{6,7},{8,9},{9,10},{10,11},{11... | collective-permute-start | bytes 294920 | tf_op jit(solution)/shard_map/ppermute | solution.py:17
  109.0 17.8 %collective-permute-start.5 = (bf16[24,32,4,16]{1,3,2,0:T(8,128)(2,1)S(1)}, bf16[24,32,4,16]{1,3,2,0:T(8,128)(2,1)S(1)}, u32[]{:S(2)}, u32[]{:S(2)}) collective-permute-start(bf16[24,32,4,16]{1,3,2,0:T(8,128)(2,1)S(1)} %get-tuple-element.6), channel_id=1, source_target_pairs={{1,0},{2,1},{3,2},{4,3},{5,4},{6,5},{7,6},{9,8},{10,9},{11,10},{12... | collective-permute-start | bytes 294920 | tf_op jit(solution)/shard_map/ppermute | solution.py:19
  129.1 9.6 %copy-start.1 = (bf16[24,32,24,16]{1,3,2,0:T(8,128)(2,1)}, bf16[24,32,24,16]{1,3,2,0:T(8,128)(2,1)S(1)}, u32[]{:S(2)}) copy-start(bf16[24,32,24,16]{1,3,2,0:T(8,128)(2,1)S(1)} %pad_maximum_fusion.1) | copy-start | bytes 1769476
  146.7 34.9 %collective-permute-start.6 = (bf16[6,12,8,16]{3,2,1,0:T(8,128)(2,1)S(1)}, bf16[6,12,8,16]{3,2,1,0:T(8,128)(2,1)S(1)}, u32[]{:S(2)}, u32[]{:S(2)}) collective-permute-start(bf16[6,12,8,16]{3,2,1,0:T(8,128)(2,1)S(1)} %get-tuple-element.13), channel_id=1, source_target_pairs={{0,16},{1,17},{2,18},{3,19},{4,20},{5,21},{6,22},{7,23},{8,24},{9,... | collective-permute-start | bytes 55304 | tf_op jit(solution)/shard_map/ppermute | solution.py:17
  148.6 8.4 %copy-start.2 = (bf16[24,32,24,16]{1,3,2,0:T(8,128)(2,1)S(1)}, bf16[24,32,24,16]{1,3,2,0:T(8,128)(2,1)}, u32[]{:S(2)}) copy-start(bf16[24,32,24,16]{1,3,2,0:T(8,128)(2,1)} %copy-done.1) | copy-start | bytes 1769476
  148.6 8.4 %copy-start.13 = (bf16[32,24,24,16,1]{0,3,2,1,4:T(8,128)(2,1)S(1)}, bf16[32,24,24,16,1]{0,3,2,1,4:T(8,128)(2,1)}, u32[]{:S(2)}) copy-start(bf16[32,24,24,16,1]{0,3,2,1,4:T(8,128)(2,1)} %convert_bitcast_fusion.5) | copy-start | bytes 1769476
  148.7 33.0 %collective-permute-start.7 = (bf16[6,12,8,16]{3,2,1,0:T(8,128)(2,1)S(1)}, bf16[6,12,8,16]{3,2,1,0:T(8,128)(2,1)S(1)}, u32[]{:S(2)}, u32[]{:S(2)}) collective-permute-start(bf16[6,12,8,16]{3,2,1,0:T(8,128)(2,1)S(1)} %get-tuple-element.14), channel_id=1, source_target_pairs={{16,0},{17,1},{18,2},{19,3},{20,4},{21,5},{22,6},{23,7},{24,8},{25... | collective-permute-start | bytes 55304 | tf_op jit(solution)/shard_map/ppermute | solution.py:19
  157.1 4.9 copy-start.12
  162.0 4.9 copy-start.11
  166.9 4.8 copy-start.10
  171.7 4.8 copy-start.9
  176.5 11.2 %copy-start.8 = (bf16[32,24,24,16,1]{0,3,2,1,4:T(8,128)(2,1)S(1)}, bf16[32,24,24,16,1]{0,3,2,1,4:T(8,128)(2,1)}, u32[]{:S(2)}) copy-start(bf16[32,24,24,16,1]{0,3,2,1,4:T(8,128)(2,1)} %convert_bitcast_fusion.3) | copy-start | bytes 1769476
  181.8 10.8 %collective-permute-start.8 = (bf16[20,6,8,16]{3,2,1,0:T(8,128)(2,1)S(1)}, bf16[20,6,8,16]{3,2,1,0:T(8,128)(2,1)S(1)}, u32[]{:S(2)}, u32[]{:S(2)}) collective-permute-start(bf16[20,6,8,16]{3,2,1,0:T(8,128)(2,1)S(1)} %get-tuple-element.11), channel_id=1, source_target_pairs={{0,8},{1,9},{2,10},{3,11},{4,12},{5,13},{6,14},{7,15},{16,24},{17,... | collective-permute-start | bytes 92168 | tf_op jit(solution)/shard_map/ppermute | solution.py:17
  186.5 10.6 %collective-permute-start.9 = (bf16[20,6,8,16]{3,2,1,0:T(8,128)(2,1)S(1)}, bf16[20,6,8,16]{3,2,1,0:T(8,128)(2,1)S(1)}, u32[]{:S(2)}, u32[]{:S(2)}) collective-permute-start(bf16[20,6,8,16]{3,2,1,0:T(8,128)(2,1)S(1)} %get-tuple-element.12), channel_id=1, source_target_pairs={{8,0},{9,1},{10,2},{11,3},{12,4},{13,5},{14,6},{15,7},{24,16},{25,... | collective-permute-start | bytes 92168 | tf_op jit(solution)/shard_map/ppermute | solution.py:19
  192.6 6.4 copy-start.21
  197.1 1.9 copy-start.22
  200.6 25.5 %collective-permute-start.10 = (bf16[20,24,6,16]{1,3,2,0:T(8,128)(2,1)S(1)}, bf16[20,24,6,16]{1,3,2,0:T(8,128)(2,1)}, u32[]{:S(2)}, u32[]{:S(2)}) collective-permute-start(bf16[20,24,6,16]{1,3,2,0:T(8,128)(2,1)S(1)} %copy.43), channel_id=1, source_target_pairs={{0,1},{1,2},{2,3},{3,4},{4,5},{5,6},{6,7},{8,9},{9,10},{10,11},{11... | collective-permute-start | bytes 276488 | tf_op jit(solution)/shard_map/ppermute | solution.py:17
  208.2 20.5 %collective-permute-start.11 = (bf16[20,24,6,16]{1,3,2,0:T(8,128)(2,1)}, bf16[20,24,6,16]{1,3,2,0:T(8,128)(2,1)}, u32[]{:S(2)}, u32[]{:S(2)}) collective-permute-start(bf16[20,24,6,16]{1,3,2,0:T(8,128)(2,1)} %copy.44), channel_id=1, source_target_pairs={{1,0},{2,1},{3,2},{4,3},{5,4},{6,5},{7,6},{9,8},{10,9},{11,10},{12... | collective-permute-start | bytes 276488 | tf_op jit(solution)/shard_map/ppermute | solution.py:19
  242.9 9.0 %copy-start.27 = (f32[8]{0:T(128)S(1)}, f32[8]{0:T(128)}, u32[]{:S(2)}) copy-start(f32[8]{0:T(128)} %param.9) | copy-start | bytes 100
  297.6 3.3 copy-start.14
  300.8 1.9 copy-start.15
  302.8 1.9 copy-start.16
  304.7 1.9 copy-start.17
  306.6 2.0 copy-start.18
  308.6 1.9 copy-start.19
  310.5 1.9 copy-start.20
  785.8 3.8 copy-start.7
  785.8 3.8 copy-start.28
  787.6 1.9 copy-start.3
Sparse Core Ops, SparseCore 0:
  297.7 402.1 all-gather.1
where the time goes:
time: 821 us; the launch traced here: 811 us
  waiting for transfers between devices  417 us (51%)
  matrix products  188 us (23%)
  local copies, waits for them, and re-layouts  111 us (14%)
  blocking collectives  39.2 us (5%)
  starting transfers between devices  30.6 us (4%)
  between operations  14.3 us (2%)
  other arithmetic  11 us (1%)
    all_gather x1, waiting for transfers between devices, per_device(): piece = lax.all_gather(section, 'gz', axis=3, tiled=True)  386 us
    dot_general x18, matrix products, correlate(): jnp.einsum('xpqm,pqyz->xyzm', padded[offset:offset + out_sizes[0]], table...  74.3 us
    all_gather x1, blocking collectives, per_device(): piece = lax.all_gather(section, 'gy', axis=2, tiled=True)  37.3 us
    dot_general x18, matrix products, correlate(): jnp.einsum('bc,bpy,cqz->pqyz', kernel[offset], pick_y, pick_z, preferred_...  37 us
    convert_element_type x9, local copies, waits for them, and re-layouts, correlate(): table = jnp.einsum('bc,bpy,cqz->pqyz', kernel[offset], pick_y, pick_z, pr...  30.3 us
    dot_general x1, matrix products, per_device(): section = jnp.einsum('gkc,gijcm->gijkm', table, piece, precision=highest)  28.3 us
    ppermute x6, waiting for transfers between devices, padded_2(): lax.ppermute(tail, axis, [(i, (i + 1) % count) for i in range(ends)])  27.1 us
    all_gather x1, local copies, waits for them, and re-layouts, per_device(): piece = lax.all_gather(section, 'gz', axis=3, tiled=True)  26.4 us
  transfers between devices with their start and end apart: 13, of which 4 were waited for; matrix products, arithmetic and copies ran while one was open for 17% of the time, Pallas kernels for 0%

commit v1 on v0

--- a/solution.py
+++ b/solution.py
@@ -144,7 +144,14 @@
     piece = lax.all_gather(section, "gy", axis=2, tiled=True)
     table = gaussian_table(first_y, top_y + 6, piece.shape[2], whole_y, gauss_width)
     section = jnp.einsum("gjb,gibcm->gijcm", table, piece, precision=highest)
-    piece = lax.all_gather(section, "gz", axis=3, tiled=True)
+    finding, everything = (lax.psum(1, "gz"), lax.axis_index("gz"))
+    piece, h_now = (section, 1)
+    while h_now < finding:
+        opened = lax.ppermute(piece, "gz", [(p, p ^ h_now) for p in range(finding)])
+        y2 = jnp.concatenate([piece, opened], axis=3)
+        reached = jnp.concatenate([opened, piece], axis=3)
+        piece = jnp.where(everything & h_now == 0, y2, reached)
+        h_now = 2 * h_now
     table = gaussian_table(first_z, top_z + 6, piece.shape[3], whole_z, gauss_width)
     section = jnp.einsum("gkc,gijcm->gijkm", table, piece, precision=highest)
     phi_top = jnp.sum(section, axis=0)

time: 821 us -> 887 us (1.080)
  waiting for transfers between devices: 417 us -> 461 us
  local copies, waits for them, and re-layouts: 111 us -> 143 us
  other arithmetic: 11 us -> 32.2 us
  between operations: 14.3 us -> 1.08 us
  matrix products: 188 us -> 175 us
  blocking collectives: 39.2 us -> 26.4 us
    ppermute x0 -> x3, waiting for transfers between devices: none -> 430 us  [per_device(): opened = lax.ppermute(piece, 'gz', [(p, p ^ h_now) for p in range(finding)])]
    all_gather x1 -> x0, waiting for transfers between devices: 386 us -> none  [per_device(): piece = lax.all_gather(section, 'gz', axis=3, tiled=True)]
    select_n x0 -> x3, local copies, waits for them, and re-layouts: none -> 33.6 us  [per_device(): piece = jnp.where(everything & h_now == 0, y2, reached)]
    all_gather x1 -> x0, local copies, waits for them, and re-layouts: 26.4 us -> none  [per_device(): piece = lax.all_gather(section, 'gz', axis=3, tiled=True)]
    ppermute x0 -> x3, local copies, waits for them, and re-layouts: none -> 20.4 us  [per_device(): opened = lax.ppermute(piece, 'gz', [(p, p ^ h_now) for p in range(finding)])]
    select_n x0 -> x2, other arithmetic: none -> 19.3 us  [per_device(): piece = jnp.where(everything & h_now == 0, y2, reached)]
    dot_general x1, matrix products: 28.3 us -> 15.3 us  [per_device(): section = jnp.einsum('gkc,gijcm->gijkm', table, piece, precision=highest)]
    all_gather x1, blocking collectives: 37.3 us -> 24.5 us  [per_device(): piece = lax.all_gather(section, 'gy', axis=2, tiled=True)]
  transfers between devices with their start and end apart: 13 -> 15, of which waited for: 4 -> 6; matrix products, arithmetic and copies ran while one was open for 17% -> 18% of each run, Pallas kernels for 0% -> 0%
where the time goes in v1:
time: 887 us; the launch traced here: 876 us
  waiting for transfers between devices  461 us (52%)
  matrix products  175 us (20%)
  local copies, waits for them, and re-layouts  143 us (16%)
  starting transfers between devices  37.2 us (4%)
  other arithmetic  32.2 us (4%)
  blocking collectives  26.4 us (3%)
    ppermute x3, waiting for transfers between devices, per_device(): opened = lax.ppermute(piece, 'gz', [(p, p ^ h_now) for p in range(finding)])  430 us
    dot_general x18, matrix products, correlate(): jnp.einsum('xpqm,pqyz->xyzm', padded[offset:offset + out_sizes[0]], table...  77.1 us
    dot_general x18, matrix products, correlate(): jnp.einsum('bc,bpy,cqz->pqyz', kernel[offset], pick_y, pick_z, preferred_...  37 us
    select_n x3, local copies, waits for them, and re-layouts, per_device(): piece = jnp.where(everything & h_now == 0, y2, reached)  33.6 us
    convert_element_type x9, local copies, waits for them, and re-layouts, correlate(): table = jnp.einsum('bc,bpy,cqz->pqyz', kernel[offset], pick_y, pick_z, pr...  30.4 us
    ppermute x6, waiting for transfers between devices, padded_2(): lax.ppermute(tail, axis, [(i, (i + 1) % count) for i in range(ends)])  26.6 us
    all_gather x1, blocking collectives, per_device(): piece = lax.all_gather(section, 'gy', axis=2, tiled=True)  24.5 us
    ppermute x6, starting transfers between devices, padded_2(): lax.ppermute(tail, axis, [(i, (i + 1) % count) for i in range(ends)])  22.6 us
  transfers between devices with their start and end apart: 15, of which 6 were waited for; matrix products, arithmetic and copies ran while one was open for 18% of the time, Pallas kernels for 0%

profile of v1, /device:TPU:0, one launch (start us, length us, event | category | flops | bytes accessed | tf_op | source)
XLA Modules:
  0.0 876.1 jit_solution(8756032401045333630)
XLA Ops:
  49.4 4.9 collective-permute-start.2
  59.1 3.8 copy.128
  62.9 3.6 copy.132
  69.3 3.8 copy.140
  73.1 3.7 copy.144
  79.4 3.8 copy.152
  83.2 3.7 copy.156
  89.6 3.9 copy.21
  93.5 4.6 copy.22
  105.5 15.9 %collective-permute-done.4 = bf16[24,32,4,16]{1,3,2,0:T(8,128)(2,1)S(1)} collective-permute-done((bf16[24,32,4,16]{1,3,2,0:T(8,128)(2,1)S(1)}, bf16[24,32,4,16]{1,3,2,0:T(8,128)(2,1)S(1)}, u32[]{:S(2)}, u32[]{:S(2)}) %collective-permute-start.4) | collective-permute-done | bytes 98336 | tf_op jit(solution)/shard_map/ppermute | solution.py:17
  125.7 7.8 fusion.62
  133.5 7.4 fusion.209
  145.0 6.6 fusion.10
  151.7 4.8 fusion.12
  156.5 4.8 fusion.14
  161.3 4.9 fusion.16
  166.2 4.8 fusion.18
  171.0 5.2 fusion.20
  176.4 4.7 collective-permute-start.8
  182.4 4.9 fusion.8
  187.3 4.4 collective-permute-done.9
  195.3 5.2 collective-permute-start.10
  204.1 6.0 fusion.6
  210.1 10.8 %collective-permute-done.10 = bf16[20,24,6,16]{1,3,2,0:T(8,128)(2,1)} collective-permute-done((bf16[20,24,6,16]{1,3,2,0:T(8,128)(2,1)S(1)}, bf16[20,24,6,16]{1,3,2,0:T(8,128)(2,1)}, u32[]{:S(2)}, u32[]{:S(2)}) %collective-permute-start.10) | collective-permute-done | bytes 92192 | tf_op jit(solution)/shard_map/ppermute | solution.py:17
  225.8 5.7 pad_maximum_fusion
  231.6 6.0 copy.65
  239.6 4.7 convolution_bitcast_fusion.1
  247.4 24.5 %all_gather.7 = f32[8,10,12,4,16]{4,0,3,1,2:T(8,128)S(1)} all-gather(f32[8,10,6,4,16]{4,0,3,1,2:T(8,128)S(1)} %fusion.103), channel_id=1, replica_groups=mesh['gx'=2,'gy'=2,'gz'=8] {'gy'}, dimensions={2}, use_global_device_ids=true | all-gather | bytes 368640 | tf_op jit(solution)/shard_map/all_gather | solution.py:144
  271.9 5.2 fusion.35
  277.1 3.7 copy.71
  283.4 3.7 fusion.54
  294.9 31.2 %collective-permute-done.12 = f32[8,10,12,4,16]{4,0,3,2,1:T(8,128)} collective-permute-done((f32[8,10,12,4,16]{4,0,3,2,1:T(8,128)}, f32[8,10,12,4,16]{4,0,3,2,1:T(8,128)}, u32[]{:S(2)}, u32[]{:S(2)}) %collective-permute-start.12) | collective-permute-done | bytes 245792 | tf_op jit(solution)/shard_map/ppermute | solution.py:150
  326.0 4.3 copy.72
  330.3 5.3 maximum_select_fusion.2
  335.7 7.4 copy.74
  347.8 81.1 %collective-permute-done.13 = f32[8,10,12,8,16]{4,3,2,1,0:T(8,128)} collective-permute-done((f32[8,10,12,8,16]{4,3,2,1,0:T(8,128)}, f32[8,10,12,8,16]{4,3,2,1,0:T(8,128)}, u32[]{:S(2)}, u32[]{:S(2)}) %collective-permute-start.13) | collective-permute-done | bytes 491552 | tf_op jit(solution)/shard_map/ppermute | solution.py:150
  428.9 7.0 copy.75
  436.0 13.9 %maximum_select_fusion = f32[8,10,12,16,16]{2,4,3,1,0:T(8,128)} fusion(f32[8,10,12,8,16]{2,4,3,1,0:T(8,128)} %copy.75, f32[8,10,12,8,16]{2,4,3,1,0:T(8,128)} %maximum_select_fusion.2, pred[]{:T(512)S(6)} %eq.413), kind=kLoop, calls=%fused_computation | loop fusion | flops 737280 | bytes 1966081 | tf_op jit(solution)/shard_map/jit(_where)/select_n | solution.py:153
  449.9 13.1 %copy.77 = f32[8,10,12,16,16]{4,3,2,1,0:T(8,128)} copy(f32[8,10,12,16,16]{2,4,3,1,0:T(8,128)} %maximum_select_fusion) | data formatting | bytes 1966080 | tf_op jit(solution)/shard_map/jit(_where)/select_n | solution.py:153
  470.5 13.1 %copy.78 = f32[8,10,12,16,16]{3,4,2,1,0:T(8,128)} copy(f32[8,10,12,16,16]{2,4,3,1,0:T(8,128)} %maximum_select_fusion) | data formatting | bytes 1966080 | tf_op jit(solution)/shard_map/jit(_where)/select_n | solution.py:153
  483.6 318.1 %collective-permute-done.14 = f32[8,10,12,16,16]{4,3,2,1,0:T(8,128)} collective-permute-done((f32[8,10,12,16,16]{4,3,2,1,0:T(8,128)}, f32[8,10,12,16,16]{4,3,2,1,0:T(8,128)}, u32[]{:S(2)}, u32[]{:S(2)}) %collective-permute-start.14) | collective-permute-done | bytes 983072 | tf_op jit(solution)/shard_map/ppermute | solution.py:150
  801.7 9.1 %copy.79 = f32[8,10,12,16,16]{3,4,2,1,0:T(8,128)} copy(f32[8,10,12,16,16]{4,3,2,1,0:T(8,128)} %collective-permute-done.14) | data formatting | bytes 1966080 | tf_op jit(solution)/shard_map/ppermute | solution.py:150
  810.8 15.3 %fusion.65 = f32[10,12,10,16]{2,3,0,1:T(8,128)} fusion(f32[8]{0:T(128)S(1)} %sqrt.6, f32[8]{0:T(128)S(1)} %copy-done.27, f32[10,32]{1,0:T(8,128)S(1)} %subtract_convert_fusion, pred[10]{0:T(512)(128)(4,1)S(1)} %copy-done.30, f32[8,10,12,16,16]{3,4,2,1,0:T(8,128)} %copy.79, f32[8,10,12,16,16]{3,4,2,1,0:T(8,128)} %copy.78, pred[]{:T(512)S(6)} %eq.412), kind=kOutput, calls=%fused_computation.110 | convolution fusion | flops 60469760 | bytes 2044235 | tf_op jit(solution)/shard_map/gkc,gijcm->gijkm/dot_general | solution.py:156
  834.6 3.5 copy.85
  838.2 3.9 fusion.173
  842.1 3.9 copy.86
  846.0 5.7 fusion.80
  861.1 9.8 %bitcast_add_fusion = f32[16,24,16,16]{1,3,0,2:T(8,128)} fusion(f32[24,16,16,16,1]{0,3,4,2,1:T(8,128)} %fusion.6, f32[24,16,16,16,1]{0,3,4,2,1:T(8,128)} %fusion.8, f32[24,16,16,16,1]{0,3,4,2,1:T(8,128)S(1)} %copy-done.32, f32[24,16,16,16,1]{0,3,4,2,1:T(8,128)} %fusion.12, f32[24,16,16,16,1]{0,3,4,2,1:T(8,128)} %fusion.14, ...), kind=kOutput, calls=%fused_computation.38 | convolution fusion | flops 151879680 | bytes 11272192 | tf_op jit(solution)/shard_map/xpqm,pqyz->xyzm/dot_general | solution.py:88
  (178 shorter events, 141.5 us)
Async XLA Ops:
  0.0 8.0 copy-start.25
  1.0 42.6 %collective-permute-start = (bf16[4,24,16,16]{1,3,2,0:T(8,128)(2,1)S(1)}, bf16[4,24,16,16]{1,3,2,0:T(8,128)(2,1)S(1)}, u32[]{:S(2)}, u32[]{:S(2)}) collective-permute-start(bf16[4,24,16,16]{1,3,2,0:T(8,128)(2,1)S(1)} %bitcast.631), channel_id=1, source_target_pairs={{0,16},{1,17},{2,18},{3,19},{4,20},{5,21},{6,22},{7,23},{8,24},{9,... | collective-permute-start | bytes 147464 | tf_op jit(solution)/shard_map/ppermute | solution.py:17
  3.6 40.0 %collective-permute-start.1 = (bf16[4,24,16,16]{1,3,2,0:T(8,128)(2,1)S(1)}, bf16[4,24,16,16]{1,3,2,0:T(8,128)(2,1)S(1)}, u32[]{:S(2)}, u32[]{:S(2)}) collective-permute-start(bf16[4,24,16,16]{1,3,2,0:T(8,128)(2,1)S(1)} %bitcast.632), channel_id=1, source_target_pairs={{16,0},{17,1},{18,2},{19,3},{20,4},{21,5},{22,6},{23,7},{24,8},{25... | collective-permute-start | bytes 147464 | tf_op jit(solution)/shard_map/ppermute | solution.py:19
  16.8 5.5 copy-start.26
  38.3 4.6 copy-start.27
  38.3 4.7 copy-start.28
  38.3 4.8 copy-start.24
  49.4 40.2 %collective-permute-start.2 = (bf16[24,4,16,16]{0,3,2,1:T(8,128)(2,1)S(1)}, bf16[24,4,16,16]{0,3,2,1:T(8,128)(2,1)}, u32[]{:S(2)}, u32[]{:S(2)}) collective-permute-start(bf16[24,4,16,16]{0,3,2,1:T(8,128)(2,1)S(1)} %copy.19), channel_id=1, source_target_pairs={{0,8},{1,9},{2,10},{3,11},{4,12},{5,13},{6,14},{7,15},{16,24},{17,... | collective-permute-start | bytes 147464 | tf_op jit(solution)/shard_map/ppermute | solution.py:17
  57.2 36.4 %collective-permute-start.3 = (bf16[24,4,16,16]{0,3,2,1:T(8,128)(2,1)}, bf16[24,4,16,16]{0,3,2,1:T(8,128)(2,1)}, u32[]{:S(2)}, u32[]{:S(2)}) collective-permute-start(bf16[24,4,16,16]{0,3,2,1:T(8,128)(2,1)} %copy.20), channel_id=1, source_target_pairs={{8,0},{9,1},{10,2},{11,3},{12,4},{13,5},{14,6},{15,7},{24,16},{25,... | collective-permute-start | bytes 147464 | tf_op jit(solution)/shard_map/ppermute | solution.py:19
  59.1 7.5 copy-start.9
  69.2 7.5 copy-start.8
  79.4 7.5 copy-start.7
  98.1 23.2 %copy-start = (bf16[24,4,16,16]{1,3,2,0:T(8,128)(2,1)S(1)}, bf16[24,4,16,16]{1,3,2,0:T(8,128)(2,1)}, u32[]{:S(2)}) copy-start(bf16[24,4,16,16]{1,3,2,0:T(8,128)(2,1)} %copy.22) | copy-start | bytes 147460
  100.1 21.2 %collective-permute-start.4 = (bf16[24,32,4,16]{1,3,2,0:T(8,128)(2,1)S(1)}, bf16[24,32,4,16]{1,3,2,0:T(8,128)(2,1)S(1)}, u32[]{:S(2)}, u32[]{:S(2)}) collective-permute-start(bf16[24,32,4,16]{1,3,2,0:T(8,128)(2,1)S(1)} %get-tuple-element.5), channel_id=1, source_target_pairs={{0,1},{1,2},{2,3},{3,4},{4,5},{5,6},{6,7},{8,9},{9,10},{10,11},{11... | collective-permute-start | bytes 294920 | tf_op jit(solution)/shard_map/ppermute | solution.py:17
  103.6 17.8 %collective-permute-start.5 = (bf16[24,32,4,16]{1,3,2,0:T(8,128)(2,1)S(1)}, bf16[24,32,4,16]{1,3,2,0:T(8,128)(2,1)S(1)}, u32[]{:S(2)}, u32[]{:S(2)}) collective-permute-start(bf16[24,32,4,16]{1,3,2,0:T(8,128)(2,1)S(1)} %get-tuple-element.6), channel_id=1, source_target_pairs={{1,0},{2,1},{3,2},{4,3},{5,4},{6,5},{7,6},{9,8},{10,9},{11,10},{12... | collective-permute-start | bytes 294920 | tf_op jit(solution)/shard_map/ppermute | solution.py:19
  123.9 9.6 %copy-start.4 = (bf16[24,32,24,16]{1,3,2,0:T(8,128)(2,1)}, bf16[24,32,24,16]{1,3,2,0:T(8,128)(2,1)S(1)}, u32[]{:S(2)}) copy-start(bf16[24,32,24,16]{1,3,2,0:T(8,128)(2,1)S(1)} %pad_maximum_fusion.1) | copy-start | bytes 1769476
  141.5 34.7 %collective-permute-start.6 = (bf16[6,12,8,16]{3,2,1,0:T(8,128)(2,1)S(1)}, bf16[6,12,8,16]{3,2,1,0:T(8,128)(2,1)S(1)}, u32[]{:S(2)}, u32[]{:S(2)}) collective-permute-start(bf16[6,12,8,16]{3,2,1,0:T(8,128)(2,1)S(1)} %get-tuple-element.13), channel_id=1, source_target_pairs={{0,16},{1,17},{2,18},{3,19},{4,20},{5,21},{6,22},{7,23},{8,24},{9,... | collective-permute-start | bytes 55304 | tf_op jit(solution)/shard_map/ppermute | solution.py:17
  143.4 8.2 copy-start.5
  143.4 8.2 copy-start.16
  143.4 32.8 %collective-permute-start.7 = (bf16[6,12,8,16]{3,2,1,0:T(8,128)(2,1)S(1)}, bf16[6,12,8,16]{3,2,1,0:T(8,128)(2,1)S(1)}, u32[]{:S(2)}, u32[]{:S(2)}) collective-permute-start(bf16[6,12,8,16]{3,2,1,0:T(8,128)(2,1)S(1)} %get-tuple-element.14), channel_id=1, source_target_pairs={{16,0},{17,1},{18,2},{19,3},{20,4},{21,5},{22,6},{23,7},{24,8},{25... | collective-permute-start | bytes 55304 | tf_op jit(solution)/shard_map/ppermute | solution.py:19
  151.7 4.8 copy-start.15
  156.5 4.8 copy-start.14
  161.3 4.9 copy-start.13
  166.2 4.8 copy-start.12
  171.0 11.4 %copy-start.11 = (bf16[32,24,24,16,1]{0,3,2,1,4:T(8,128)(2,1)S(1)}, bf16[32,24,24,16,1]{0,3,2,1,4:T(8,128)(2,1)}, u32[]{:S(2)}) copy-start(bf16[32,24,24,16,1]{0,3,2,1,4:T(8,128)(2,1)} %convert_bitcast_fusion.2) | copy-start | bytes 1769476
  176.4 10.9 %collective-permute-start.8 = (bf16[20,6,8,16]{3,2,1,0:T(8,128)(2,1)S(1)}, bf16[20,6,8,16]{3,2,1,0:T(8,128)(2,1)S(1)}, u32[]{:S(2)}, u32[]{:S(2)}) collective-permute-start(bf16[20,6,8,16]{3,2,1,0:T(8,128)(2,1)S(1)} %get-tuple-element.11), channel_id=1, source_target_pairs={{0,8},{1,9},{2,10},{3,11},{4,12},{5,13},{6,14},{7,15},{16,24},{17,... | collective-permute-start | bytes 92168 | tf_op jit(solution)/shard_map/ppermute | solution.py:17
  181.1 10.6 %collective-permute-start.9 = (bf16[20,6,8,16]{3,2,1,0:T(8,128)(2,1)S(1)}, bf16[20,6,8,16]{3,2,1,0:T(8,128)(2,1)S(1)}, u32[]{:S(2)}, u32[]{:S(2)}) collective-permute-start(bf16[20,6,8,16]{3,2,1,0:T(8,128)(2,1)S(1)} %get-tuple-element.12), channel_id=1, source_target_pairs={{8,0},{9,1},{10,2},{11,3},{12,4},{13,5},{14,6},{15,7},{24,16},{25,... | collective-permute-start | bytes 92168 | tf_op jit(solution)/shard_map/ppermute | solution.py:19
  187.3 6.3 copy-start.22
  191.7 1.9 copy-start.23
  195.3 25.6 %collective-permute-start.10 = (bf16[20,24,6,16]{1,3,2,0:T(8,128)(2,1)S(1)}, bf16[20,24,6,16]{1,3,2,0:T(8,128)(2,1)}, u32[]{:S(2)}, u32[]{:S(2)}) collective-permute-start(bf16[20,24,6,16]{1,3,2,0:T(8,128)(2,1)S(1)} %copy.43), channel_id=1, source_target_pairs={{0,1},{1,2},{2,3},{3,4},{4,5},{5,6},{6,7},{8,9},{9,10},{10,11},{11... | collective-permute-start | bytes 276488 | tf_op jit(solution)/shard_map/ppermute | solution.py:17
  202.8 20.5 %collective-permute-start.11 = (bf16[20,24,6,16]{1,3,2,0:T(8,128)(2,1)}, bf16[20,24,6,16]{1,3,2,0:T(8,128)(2,1)}, u32[]{:S(2)}, u32[]{:S(2)}) collective-permute-start(bf16[20,24,6,16]{1,3,2,0:T(8,128)(2,1)} %copy.44), channel_id=1, source_target_pairs={{1,0},{2,1},{3,2},{4,3},{5,4},{6,5},{7,6},{9,8},{10,9},{11,10},{12... | collective-permute-start | bytes 276488 | tf_op jit(solution)/shard_map/ppermute | solution.py:19
  231.5 6.0 copy-start.1
  280.9 6.3 copy-start.2
  280.9 6.3 copy-start.18
  280.9 45.2 %collective-permute-start.12 = (f32[8,10,12,4,16]{4,0,3,2,1:T(8,128)}, f32[8,10,12,4,16]{4,0,3,2,1:T(8,128)}, u32[]{:S(2)}, u32[]{:S(2)}) collective-permute-start(f32[8,10,12,4,16]{4,0,3,2,1:T(8,128)} %copy.71), channel_id=1, source_target_pairs={{0,1},{1,0},{2,3},{3,2},{4,5},{5,4},{6,7},{7,6},{8,9},{9,8},{10,11... | collective-permute-start | bytes 737288 | tf_op jit(solution)/shard_map/ppermute | solution.py:150
  287.2 2.0 copy-start.19
  289.1 1.9 copy-start.20
  291.1 1.9 copy-start.21
  335.7 9.0 %copy-start.3 = (bf16[20,24,20,16]{3,2,1,0:T(8,128)(2,1)S(1)}, bf16[20,24,20,16]{3,2,1,0:T(8,128)(2,1)}, u32[]{:S(2)}) copy-start(bf16[20,24,20,16]{3,2,1,0:T(8,128)(2,1)} %copy-done.1) | copy-start | bytes 921604
  343.0 85.9 %collective-permute-start.13 = (f32[8,10,12,8,16]{4,3,2,1,0:T(8,128)}, f32[8,10,12,8,16]{4,3,2,1,0:T(8,128)}, u32[]{:S(2)}, u32[]{:S(2)}) collective-permute-start(f32[8,10,12,8,16]{4,3,2,1,0:T(8,128)} %copy.74), channel_id=1, source_target_pairs={{0,2},{1,3},{2,0},{3,1},{4,6},{5,7},{6,4},{7,5},{8,10},{9,11},{10,... | collective-permute-start | bytes 1474568 | tf_op jit(solution)/shard_map/ppermute | solution.py:150
  463.0 5.6 copy-start.17
  463.0 338.7 %collective-permute-start.14 = (f32[8,10,12,16,16]{4,3,2,1,0:T(8,128)}, f32[8,10,12,16,16]{4,3,2,1,0:T(8,128)}, u32[]{:S(2)}, u32[]{:S(2)}) collective-permute-start(f32[8,10,12,16,16]{4,3,2,1,0:T(8,128)} %copy.77), channel_id=1, source_target_pairs={{0,4},{1,5},{2,6},{3,7},{4,0},{5,1},{6,2},{7,3},{8,12},{9,13},{10,... | collective-permute-start | bytes 2949128 | tf_op jit(solution)/shard_map/ppermute | solution.py:150
  483.6 327.1 %copy-start.30 = (pred[10]{0:T(512)(128)(4,1)S(1)}, pred[10]{0:T(512)(128)(4,1)}, u32[]{:S(2)}) copy-start(pred[10]{0:T(512)(128)(4,1)} %compare_and_fusion) | copy-start | bytes 34
  842.1 3.9 copy-start.31
  854.6 2.7 copy-start.29
  857.3 3.8 copy-start.10
  857.3 3.8 copy-start.32
  859.2 1.9 copy-start.6
